TPU v7x, 32 devices: a whole 2x2x4 slice. The times are simulated.
32 devices in a mesh: group: 2 (over y), seq: 4 (over z), batch: 2 (over x), chan: 2 (over core).
Axes of the slice: x: 2, y: 2, z: 4, core: 2. Of those that a mesh axis runs over, the one named last changes fastest.
Arguments:
- seq_in: bfloat16 [4, 4096, 768], P(('group', 'batch'), 'seq', 'chan'), parts along dimension 0, may hold values from -6 to 6
- conv_weight: bfloat16 [3, 768, 768], P(None, 'chan'), may hold values from -0.125 to 0.125
- cotangent: bfloat16 [4, 2048, 768], P(('group', 'batch'), 'seq', 'chan'), parts along dimension 0, may hold values from -0.59765625 to 0.59765625
Outputs:
- block_out: bfloat16 [4, 2048, 768], P(('group', 'batch'), 'seq', 'chan'), parts along dimension 0
- input_grad: bfloat16 [4, 4096, 768], P(('group', 'batch'), 'seq', 'chan'), parts along dimension 0
- weight_grad: float32 [6, 768, 768], P('group', 'chan', 'batch'), parts along dimension 0
There are 2 independent parts, one for each index of `group`. A program takes and returns all parts, laid end to end along the dimension named above; an argument that names none is the same for every part. Nothing has to cross between parts.
All inputs are finite; a program needn't handle non-finite values.
Results may differ from a plain program's by a relative error of at most 0.0031.
Values may be sent and summed in bfloat16 or wider, within the bound.
No kernel may reach another device: no remote copies, remote signals or barrier semaphores. Data moves between devices by JAX's collectives and lax.ppermute only.
A program may use at most 64 MiB of HBM per device.

v0:
```python
import jax
import jax.numpy as jnp
from jax import lax
from jax.sharding import PartitionSpec as P


def shift_from(block, axis, distance):
    size = lax.axis_size(axis)
    route = [(i - distance, i) for i in range(size) if 0 <= i - distance < size]
    return lax.ppermute(block, axis, route)


def half_of(array, index, axis):
    parts = 2
    shape = array.shape
    split = shape[:axis] + (parts, shape[axis] // parts) + shape[axis + 1 :]
    return lax.dynamic_index_in_dim(array.reshape(split), index, axis, keepdims=False)


def shards(seq_in, conv_weight, cotangent):
    local_in = seq_in[0]
    local_cot = cotangent[0]
    rows = local_in.shape[0] // 2
    width = local_in.shape[1]
    spread = rows // 2
    pooled = 0.5 * jnp.sum(local_in.astype(jnp.float32).reshape(rows, 2, width), axis=1)
    activation = jax.nn.gelu(pooled).astype(jnp.bfloat16)
    both = jnp.stack([activation, local_cot])
    from_prev = shift_from(both[:, rows - spread :], "seq", 1)
    from_next = shift_from(both[:, :spread], "seq", -1)
    own_ext = jnp.concatenate([from_prev, both, from_next], 1)
    full_ext = lax.all_gather(own_ext, "chan", axis=2, tiled=True)
    act_full, cot_full = (full_ext[0], full_ext[1])
    weight_cols = lax.all_to_all(conv_weight, "chan", 2, 1, tiled=True)
    act_taps = jnp.stack([act_full[k * spread : k * spread + rows] for k in range(3)], 1)
    conv_out = jnp.dot(
        act_taps.reshape(rows, -1),
        weight_cols.reshape(-1, weight_cols.shape[2]),
        preferred_element_type=jnp.float32,
    )
    block_out = (pooled + conv_out).astype(jnp.bfloat16)
    cot_taps = jnp.stack(
        [cot_full[(2 - k) * spread : (2 - k) * spread + rows] for k in range(3)], 1
    )
    activ_grad = jnp.einsum(
        "tko,kio->ti", cot_taps, conv_weight, preferred_element_type=jnp.float32
    )
    unused, gelu_back = jax.vjp(jax.nn.gelu, pooled)
    pooled_grad = local_cot.astype(jnp.float32) + gelu_back(activ_grad)[0]
    input_grad = jnp.repeat(0.5 * pooled_grad, 2, axis=0).astype(jnp.bfloat16)
    own_taps = jnp.stack([own_ext[0, k * spread : k * spread + rows] for k in range(3)], 1)
    cot_mid = cot_full[spread : spread + rows]
    batch_count = lax.axis_size("batch")
    if batch_count == 2:
        b = lax.axis_index("batch")
        send = jnp.einsum(
            "tki,to->kio", own_taps, half_of(cot_mid, 1 - b, 1), preferred_element_type=jnp.float32
        )
        keep = jnp.einsum(
            "tki,to->kio", own_taps, half_of(cot_mid, b, 1), preferred_element_type=jnp.float32
        )
        summed = keep + lax.ppermute(send, "batch", [(0, 1), (1, 0)])
    else:
        partial = jnp.einsum("tki,to->kio", own_taps, cot_mid, preferred_element_type=jnp.float32)
        summed = lax.psum_scatter(partial, "batch", scatter_dimension=2, tiled=True)
    weight_grad = lax.psum(summed, "seq")
    return (block_out[None], input_grad[None], weight_grad)


def solution(mesh):
    in_specs = (
        P(("group", "batch"), "seq", "chan"),
        P(None, "chan", None),
        P(("group", "batch"), "seq", "chan"),
    )
    out_specs = (
        P(("group", "batch"), "seq", "chan"),
        P(("group", "batch"), "seq", "chan"),
        P("group", "chan", "batch"),
    )
    return jax.shard_map(shards, mesh=mesh, in_specs=in_specs, out_specs=out_specs, check_vma=False)
```

profile of v0, /device:TPU:0, one launch (start us, length us, event | category | flops | bytes accessed | tf_op | source)
XLA Modules:
  0.0 179.5 jit_solution(5351627847527597983)
XLA Ops:
  7.2 2.2 %reshape.129 = f32[512,2,384]{2,1,0:T(2,128)S(1)} reshape(bf16[1,1024,384]{2,1,0:T(8,128)(2,1)} %param.3) | data formatting | bytes 2359296 | tf_op jit(solution)/shard_map/convert_element_type | solution.py:26
  9.4 1.9 %reduce_sum.9 = f32[512,384]{1,0:T(8,128)S(1)} reduce(f32[512,2,384]{2,1,0:T(2,128)S(1)} %reshape.129, f32[]{:T(128)} %constant.8.clone.1), dimensions={1}, to_apply=%region_0.0 | reduce | flops 196608 | bytes 2359300 | tf_op jit(solution)/shard_map/reduce_sum | solution.py:26
  11.3 0.3 fusion.27
  11.6 0.1 fusion.39
  11.7 5.0 %collective-permute-start = (bf16[2,256,384]{2,1,0:T(8,128)(2,1)S(1)}, bf16[2,256,384]{2,1,0:T(8,128)(2,1)S(1)}, u32[]{:S(2)}, u32[]{:S(2)}) collective-permute-start(bf16[2,256,384]{2,1,0:T(8,128)(2,1)S(1)} %get-tuple-element.14), channel_id=1, source_target_pairs={{0,4},{4,8},{8,12},{1,5},{5,9},{9,13},{2,6},{6,10},{10,14},{3,7},{... | collective-permute-start | bytes 1179656 | tf_op jit(solution)/shard_map/ppermute | solution.py:10
  16.7 1.3 collective-permute-start.1
  18.0 7.0 %collective-permute-done = bf16[2,256,384]{2,1,0:T(8,128)(2,1)S(1)} collective-permute-done((bf16[2,256,384]{2,1,0:T(8,128)(2,1)S(1)}, bf16[2,256,384]{2,1,0:T(8,128)(2,1)S(1)}, u32[]{:S(2)}, u32[]{:S(2)}) %collective-permute-start) | collective-permute-done | bytes 393248 | tf_op jit(solution)/shard_map/ppermute | solution.py:10
  25.0 4.1 %collective-permute-done.1 = bf16[2,256,384]{2,1,0:T(8,128)(2,1)S(1)} collective-permute-done((bf16[2,256,384]{2,1,0:T(8,128)(2,1)S(1)}, bf16[2,256,384]{2,1,0:T(8,128)(2,1)S(1)}, u32[]{:S(2)}, u32[]{:S(2)}) %collective-permute-start.1) | collective-permute-done | bytes 393248 | tf_op jit(solution)/shard_map/ppermute | solution.py:10
  29.1 1.3 pad_maximum_fusion.1
  30.5 0.0 all-reduce.2.cloned.1.call-start
  30.5 1.0 fusion.35
  31.6 0.1 fusion.41
  31.6 11.2 %all-gather.2.cloned.1.call-done = bf16[2,1024,768]{2,1,0:T(8,128)(2,1)} async-done(((bf16[2,1024,384]{2,1,0:T(8,128)(2,1)}), bf16[2,1024,768]{2,1,0:T(8,128)(2,1)}) %all-gather.2.cloned.1.call-update) | async-done | bytes 3145744 | tf_op jit(solution)/shard_map/all_gather | solution.py:32
  42.8 4.6 %fusion.45 = (bf16[1,512,768]{2,1,0:T(8,128)(2,1)S(1)}, bf16[512,1,768]{2,0,1:T(8,128)(2,1)}, bf16[512,1,768]{2,0,1:T(8,128)(2,1)}, bf16[512,1,768]{2,0,1:T(8,12...) fusion(bf16[2,1024,768]{2,1,0:T(8,128)(2,1)} %all-gather.2.cloned.1.call-done), kind=kLoop, calls=%fused_computation.67 | loop fusion | bytes 10223616 | tf_op jit(solution)/shard_map/slice | solution.py:43
  47.4 0.2 reshape.128
  47.6 1.6 constant_dynamic-slice_fusion.1
  49.3 0.8 fusion.38
  50.1 1.8 %collective-permute-start.2 = (f32[3,384,384]{2,1,0:T(8,128)S(1)}, f32[3,384,384]{2,1,0:T(8,128)S(1)}, u32[]{:S(2)}, u32[]{:S(2)}) collective-permute-start(f32[3,384,384]{2,1,0:T(8,128)S(1)} %fusion.38), channel_id=1, source_target_pairs={{0,2},{2,0},{1,3},{3,1},{4,6},{6,4},{5,7},{7,5},{8,10},{10,8},{9,1... | collective-permute-start | bytes 5308424 | tf_op jit(solution)/shard_map/ppermute | solution.py:62
  51.9 39.1 %collective-permute-done.2 = f32[3,384,384]{2,1,0:T(8,128)S(1)} collective-permute-done((f32[3,384,384]{2,1,0:T(8,128)S(1)}, f32[3,384,384]{2,1,0:T(8,128)S(1)}, u32[]{:S(2)}, u32[]{:S(2)}) %collective-permute-start.2) | collective-permute-done | bytes 1769504 | tf_op jit(solution)/shard_map/ppermute | solution.py:62
  91.0 2.0 %convolution_add_fusion = f32[3,384,384]{2,1,0:T(8,128)} fusion(f32[3,384,384]{2,1,0:T(8,128)S(1)} %collective-permute-done.2, bf16[512,1,384]{2,0,1:T(8,128)(2,1)S(1)} %get-tuple-element.13, bf16[512,1,384]{2,0,1:T(8,128)(2,1)S(1)} %copy-done.1, bf16[512,1,384]{2,0,1:T(8,128)(2,1)S(1)} %get-tuple-element.12, bf16[512,1,384]{2,1,0:T(2,128)(2,1)S(1)} %get-tuple-element.10), kind=kOutput, calls=%fused_computation.8 | convolution fusion | flops 454606848 | bytes 5111808 | tf_op jit(solution)/shard_map/tki,to->kio/dot_general | solution.py:59
  93.0 4.0 %copy.21 = bf16[3,384,768]{1,0,2:T(4,128)(2,1)S(1)} copy(bf16[3,384,768]{2,1,0:T(8,128)(2,1)} %param.4) | data formatting | bytes 3538944 | tf_op args[1]
  97.0 5.6 %all_to_all.15 = bf16[3,384,768]{1,0,2:T(4,128)(2,1)S(1)} all-to-all(bf16[3,384,768]{1,0,2:T(4,128)(2,1)S(1)} %copy.21), channel_id=1, replica_groups=mesh['group'=2,'seq'=4,'batch'=2,'chan'=2] {'chan'}, dimensions={2} | all-to-all | bytes 3538944 | tf_op jit(solution)/shard_map/all_to_all | solution.py:34
  102.6 0.2 copy.22
  102.9 2.3 %copy.23 = bf16[3,2,384,384]{3,2,1,0:T(8,128)(2,1)} copy(bf16[3,2,384,384]{2,3,1,0:T(8,128)(2,1)S(1)} %bitcast.46) | data formatting | bytes 3538944 | tf_op jit(solution)/shard_map/all_to_all | solution.py:34
  105.1 4.0 %fusion.19 = bf16[512,384]{1,0:T(8,128)(2,1)S(1)} fusion(bf16[3,384,768]{2,1,0:T(8,128)(2,1)} %param.4, bf16[512,1,768]{2,0,1:T(8,128)(2,1)} %get-tuple-element.5, bf16[512,1,768]{2,0,1:T(8,128)(2,1)} %get-tuple-element.4, bf16[512,1,768]{2,0,1:T(8,128)(2,1)} %get-tuple-element.6, f32[512,384]{1,0:T(8,128)S(1)} %reduce_sum.9, ...), kind=kOutput, calls=%fused_computation.26 | convolution fusion | flops 913047552 | bytes 5701632 | tf_op jit(solution)/shard_map/tko,kio->ti/dot_general | solution.py:45
  109.2 0.4 broadcast_in_dim.8
  109.6 1.2 convert_element_type.60
  110.8 1.9 %pad_maximum_fusion = bf16[512,3,768]{2,0,1:T(8,128)(2,1)S(1)} fusion(bf16[512,1,768]{2,0,1:T(8,128)(2,1)} %get-tuple-element.7, bf16[512,1,768]{2,0,1:T(8,128)(2,1)} %get-tuple-element.8, bf16[512,1,768]{2,0,1:T(8,128)(2,1)} %get-tuple-element.9), kind=kLoop, calls=%fused_computation | loop fusion | flops 2359296 | bytes 4718592 | tf_op jit(solution)/shard_map/stack | solution.py:35
  112.7 2.5 %copy.20 = bf16[512,3,768]{0,2,1:T(8,128)(2,1)} copy(bf16[512,3,768]{2,0,1:T(8,128)(2,1)S(1)} %pad_maximum_fusion) | data formatting | bytes 4718592 | tf_op jit(solution)/shard_map/stack | solution.py:35
  115.2 4.4 %fusion.10 = bf16[1,512,384]{2,1,0:T(8,128)(2,1)} fusion(bf16[512,2304]{0,1:T(8,128)(2,1)} %bitcast.45, bf16[2304,384]{1,0:T(8,128)(2,1)} %bitcast.47, f32[512,384]{1,0:T(8,128)S(1)} %reduce_sum.9), kind=kOutput, calls=%fused_computation.12 | convolution fusion | flops 906559488 | bytes 5308416 | tf_op jit(solution)/shard_map/dot_general | solution.py:36
  119.6 50.3 %all-reduce.2.cloned.1.call-done = f32[3,384,384]{2,1,0:T(8,128)} async-done(((f32[3,384,384]{2,1,0:T(8,128)}), f32[3,384,384]{2,1,0:T(8,128)}) %all-reduce.2.cloned.1.call-update) | async-done | bytes 1769488 | tf_op jit(solution)/shard_map/psum | solution.py:66
  169.8 2.8 %copy.37 = f32[3,384,384]{2,1,0:T(8,128)} copy(f32[3,384,384]{2,1,0:T(8,128)} %all-reduce.2.cloned.1.call-done) | data formatting | bytes 3538944
  (7 shorter events, 0.1 us)
Async XLA Ops:
  7.2 35.7 %all-gather.2.cloned.1.call-start = ((), (), s32[]{:S(2)}) async-start(), calls=%async_computation.1 | async-start | bytes 4718592 | tf_op jit(solution)/shard_map/all_gather | solution.py:32
  9.4 2.2 %copy-start = (bf16[1,512,384]{2,1,0:T(8,128)(2,1)S(1)}, bf16[1,512,384]{2,1,0:T(8,128)(2,1)}, u32[]{:S(2)}) copy-start(bf16[1,512,384]{2,1,0:T(8,128)(2,1)} %param.5) | copy-start | bytes 1179652
  11.7 13.3 %collective-permute-start = (bf16[2,256,384]{2,1,0:T(8,128)(2,1)S(1)}, bf16[2,256,384]{2,1,0:T(8,128)(2,1)S(1)}, u32[]{:S(2)}, u32[]{:S(2)}) collective-permute-start(bf16[2,256,384]{2,1,0:T(8,128)(2,1)S(1)} %get-tuple-element.14), channel_id=1, source_target_pairs={{0,4},{4,8},{8,12},{1,5},{5,9},{9,13},{2,6},{6,10},{10,14},{3,7},{... | collective-permute-start | bytes 1179656 | tf_op jit(solution)/shard_map/ppermute | solution.py:10
  16.7 12.5 %collective-permute-start.1 = (bf16[2,256,384]{2,1,0:T(8,128)(2,1)S(1)}, bf16[2,256,384]{2,1,0:T(8,128)(2,1)S(1)}, u32[]{:S(2)}, u32[]{:S(2)}) collective-permute-start(bf16[2,256,384]{2,1,0:T(8,128)(2,1)S(1)} %get-tuple-element.15), channel_id=1, source_target_pairs={{4,0},{8,4},{12,8},{5,1},{9,5},{13,9},{6,2},{10,6},{14,10},{7,3},{... | collective-permute-start | bytes 1179656 | tf_op jit(solution)/shard_map/ppermute | solution.py:10
  30.5 139.4 %all-reduce.2.cloned.1.call-start = ((), (), s32[]{:S(2)}) async-start(), calls=%async_computation.2 | async-start | bytes 3538944 | tf_op jit(solution)/shard_map/psum | solution.py:66
  47.6 1.6 copy-start.1
  50.1 40.9 %collective-permute-start.2 = (f32[3,384,384]{2,1,0:T(8,128)S(1)}, f32[3,384,384]{2,1,0:T(8,128)S(1)}, u32[]{:S(2)}, u32[]{:S(2)}) collective-permute-start(f32[3,384,384]{2,1,0:T(8,128)S(1)} %fusion.38), channel_id=1, source_target_pairs={{0,2},{2,0},{1,3},{3,1},{4,6},{6,4},{5,7},{7,5},{8,10},{10,8},{9,1... | collective-permute-start | bytes 5308424 | tf_op jit(solution)/shard_map/ppermute | solution.py:62
Sparse Core Ops, SparseCore 0:
  30.6 12.2 all-gather.1
  93.2 76.6 all-reduce.1
where the time goes:
time: 180 us; the launch traced here: 179 us
  waiting for transfers between devices  112 us (62%)
  local copies, waits for them, and re-layouts  21.9 us (12%)
  between operations  14.2 us (8%)
  matrix products  11.3 us (6%)
  starting transfers between devices  8.15 us (5%)
  other arithmetic  6.57 us (4%)
  blocking collectives  5.63 us (3%)
    psum x1, waiting for transfers between devices, shards(): weight_grad = lax.psum(summed, 'seq')  50.3 us
    ppermute x1, waiting for transfers between devices, shards(): summed = keep + lax.ppermute(send, 'batch', [(0, 1), (1, 0)])  39.1 us
    all_gather x1, waiting for transfers between devices, shards(): full_ext = lax.all_gather(own_ext, 'chan', axis=2, tiled=True)  11.2 us
    ppermute x2, waiting for transfers between devices, shift_from(): return lax.ppermute(block, axis, route)  11.2 us
    unnamed x6, local copies, waits for them, and re-layouts  6.76 us
    ppermute x2, starting transfers between devices, shift_from(): return lax.ppermute(block, axis, route)  6.27 us
    all_to_all x1, blocking collectives, shards(): weight_cols = lax.all_to_all(conv_weight, 'chan', 2, 1, tiled=True)  5.63 us
    slice x1, local copies, waits for them, and re-layouts, shards(): cot_full[(2 - k) * spread:(2 - k) * spread + rows]  4.6 us
  transfers between devices with their start and end apart: 5, of which 5 were waited for; matrix products, arithmetic and copies ran while one was open for 12% of the time, Pallas kernels for 0%

commit v1 on v0

--- a/solution.py
+++ b/solution.py
@@ -63,7 +63,10 @@
     else:
         partial = jnp.einsum("tki,to->kio", own_taps, cot_mid, preferred_element_type=jnp.float32)
         summed = lax.psum_scatter(partial, "batch", scatter_dimension=2, tiled=True)
-    weight_grad = lax.psum(summed, "seq")
+    count, weight_grad = (lax.axis_size("seq"), summed)
+    for reach in [1 << k_2 for k_2 in range(count.bit_length() - 1)]:
+        swap = [(i_2, i_2 ^ reach) for i_2 in range(count)]
+        weight_grad = weight_grad + lax.ppermute(weight_grad, "seq", swap)
     return (block_out[None], input_grad[None], weight_grad)
 
 

time: 180 us -> 222 us (1.23)
  waiting for transfers between devices: 112 us -> 149 us
  other arithmetic: 6.57 us -> 11.3 us
  starting transfers between devices: 8.15 us -> 12.6 us
  local copies, waits for them, and re-layouts: 21.9 us -> 19 us
    ppermute x0 -> x2, waiting for transfers between devices: none -> 87.4 us  [shards(): weight_grad = weight_grad + lax.ppermute(weight_grad, 'seq', swap)]
    psum x1 -> x0, waiting for transfers between devices: 50.3 us -> none  [shards(): weight_grad = lax.psum(summed, 'seq')]
    add x0 -> x2, other arithmetic: none -> 4.79 us  [shards(): weight_grad = weight_grad + lax.ppermute(weight_grad, 'seq', swap)]
    ppermute x0 -> x2, starting transfers between devices: none -> 4.49 us  [shards(): weight_grad = weight_grad + lax.ppermute(weight_grad, 'seq', swap)]
    unnamed x6 -> x5, local copies, waits for them, and re-layouts: 6.76 us -> 3.96 us
  transfers between devices with their start and end apart: 5 -> 6, of which waited for: 5 -> 6; matrix products, arithmetic and copies ran while one was open for 12% -> 10% of each run, Pallas kernels for 0% -> 0%
where the time goes in v1:
time: 222 us
  waiting for transfers between devices  149 us (67%)
  local copies, waits for them, and re-layouts  19 us (9%)
  between operations  14.2 us (6%)
  starting transfers between devices  12.6 us (6%)
  other arithmetic  11.3 us (5%)
  matrix products  10 us (5%)
  blocking collectives  5.63 us (3%)
    ppermute x2, waiting for transfers between devices, shards(): weight_grad = weight_grad + lax.ppermute(weight_grad, 'seq', swap)  87.4 us
    ppermute x1, waiting for transfers between devices, shards(): summed = keep + lax.ppermute(send, 'batch', [(0, 1), (1, 0)])  39.1 us
    all_gather x1, waiting for transfers between devices, shards(): full_ext = lax.all_gather(own_ext, 'chan', axis=2, tiled=True)  11.3 us
    ppermute x2, waiting for transfers between devices, shift_from(): return lax.ppermute(block, axis, route)  11.2 us
    ppermute x2, starting transfers between devices, shift_from(): return lax.ppermute(block, axis, route)  6.27 us
    all_to_all x1, blocking collectives, shards(): weight_cols = lax.all_to_all(conv_weight, 'chan', 2, 1, tiled=True)  5.63 us
    add x2, other arithmetic, shards(): weight_grad = weight_grad + lax.ppermute(weight_grad, 'seq', swap)  4.79 us
    slice x1, local copies, waits for them, and re-layouts, shards(): cot_full[(2 - k) * spread:(2 - k) * spread + rows]  4.55 us
  transfers between devices with their start and end apart: 6, of which 6 were waited for; matrix products, arithmetic and copies ran while one was open for 10% of the time, Pallas kernels for 0%

profile of v1, /device:TPU:0, one launch (start us, length us, event | category | flops | bytes accessed | tf_op | source)
XLA Modules:
  0.0 221.7 jit_solution(17003445993316854878)
XLA Ops:
  7.2 2.2 reshape.129
  9.4 1.9 reduce_sum.9
  11.3 0.3 fusion.27
  11.7 5.0 %collective-permute-start = (bf16[2,256,384]{2,1,0:T(8,128)(2,1)S(1)}, bf16[2,256,384]{2,1,0:T(8,128)(2,1)S(1)}, u32[]{:S(2)}, u32[]{:S(2)}) collective-permute-start(bf16[2,256,384]{2,1,0:T(8,128)(2,1)S(1)} %get-tuple-element.14), channel_id=1, source_target_pairs={{0,4},{4,8},{8,12},{1,5},{5,9},{9,13},{2,6},{6,10},{10,14},{3,7},{... | collective-permute-start | bytes 1179656 | tf_op jit(solution)/shard_map/ppermute | solution.py:10
  16.7 1.3 collective-permute-start.1
  18.0 7.0 %collective-permute-done = bf16[2,256,384]{2,1,0:T(8,128)(2,1)S(1)} collective-permute-done((bf16[2,256,384]{2,1,0:T(8,128)(2,1)S(1)}, bf16[2,256,384]{2,1,0:T(8,128)(2,1)S(1)}, u32[]{:S(2)}, u32[]{:S(2)}) %collective-permute-start) | collective-permute-done | bytes 393248 | tf_op jit(solution)/shard_map/ppermute | solution.py:10
  25.0 4.1 %collective-permute-done.1 = bf16[2,256,384]{2,1,0:T(8,128)(2,1)S(1)} collective-permute-done((bf16[2,256,384]{2,1,0:T(8,128)(2,1)S(1)}, bf16[2,256,384]{2,1,0:T(8,128)(2,1)S(1)}, u32[]{:S(2)}, u32[]{:S(2)}) %collective-permute-start.1) | collective-permute-done | bytes 393248 | tf_op jit(solution)/shard_map/ppermute | solution.py:10
  29.1 1.3 pad_maximum_fusion.1
  30.5 1.0 fusion.35
  31.6 11.3 %all-gather.2.cloned.1.call-done = bf16[2,1024,768]{2,1,0:T(8,128)(2,1)} async-done(((bf16[2,1024,384]{2,1,0:T(8,128)(2,1)}), bf16[2,1024,768]{2,1,0:T(8,128)(2,1)}) %all-gather.2.cloned.1.call-update) | async-done | bytes 3145744 | tf_op jit(solution)/shard_map/all_gather | solution.py:32
  42.8 4.5 %fusion.45 = (bf16[1,512,768]{2,1,0:T(8,128)(2,1)S(1)}, bf16[512,1,768]{2,0,1:T(8,128)(2,1)}, bf16[512,1,768]{2,0,1:T(8,128)(2,1)}, bf16[512,1,768]{2,0,1:T(8,12...) fusion(bf16[2,1024,768]{2,1,0:T(8,128)(2,1)} %all-gather.2.cloned.1.call-done), kind=kLoop, calls=%fused_computation.67 | loop fusion | bytes 10223616 | tf_op jit(solution)/shard_map/slice | solution.py:43
  47.6 1.6 constant_dynamic-slice_fusion.1
  49.2 0.8 fusion.38
  50.1 1.8 collective-permute-start.2
  51.9 39.1 %collective-permute-done.2 = f32[3,384,384]{2,1,0:T(8,128)S(1)} collective-permute-done((f32[3,384,384]{2,1,0:T(8,128)S(1)}, f32[3,384,384]{2,1,0:T(8,128)S(1)}, u32[]{:S(2)}, u32[]{:S(2)}) %collective-permute-start.2) | collective-permute-done | bytes 1769504 | tf_op jit(solution)/shard_map/ppermute | solution.py:62
  90.9 0.8 convolution_add_fusion
  91.8 1.8 collective-permute-start.3
  93.6 38.2 %collective-permute-done.3 = f32[3,384,384]{2,1,0:T(8,128)S(1)} collective-permute-done((f32[3,384,384]{2,1,0:T(8,128)S(1)}, f32[3,384,384]{2,1,0:T(8,128)S(1)}, u32[]{:S(2)}, u32[]{:S(2)}) %collective-permute-start.3) | collective-permute-done | bytes 1769504 | tf_op jit(solution)/shard_map/ppermute | solution.py:69
  131.8 1.4 add.79
  133.2 2.7 %collective-permute-start.4 = (f32[3,384,384]{2,1,0:T(8,128)}, f32[3,384,384]{2,1,0:T(8,128)}, u32[]{:S(2)}, u32[]{:S(2)}) collective-permute-start(f32[3,384,384]{2,1,0:T(8,128)} %add.79), channel_id=1, source_target_pairs={{0,8},{4,12},{8,0},{12,4},{1,9},{5,13},{9,1},{13,5},{2,10},{6,14},... | collective-permute-start | bytes 5308424 | tf_op jit(solution)/shard_map/ppermute | solution.py:69
  135.9 4.0 %copy.21 = bf16[3,384,768]{1,0,2:T(4,128)(2,1)S(1)} copy(bf16[3,384,768]{2,1,0:T(8,128)(2,1)} %param.4) | data formatting | bytes 3538944 | tf_op args[1]
  139.8 5.6 %all_to_all.15 = bf16[3,384,768]{1,0,2:T(4,128)(2,1)S(1)} all-to-all(bf16[3,384,768]{1,0,2:T(4,128)(2,1)S(1)} %copy.21), channel_id=1, replica_groups=mesh['group'=2,'seq'=4,'batch'=2,'chan'=2] {'chan'}, dimensions={2} | all-to-all | bytes 3538944 | tf_op jit(solution)/shard_map/all_to_all | solution.py:34
  145.5 0.2 copy.22
  145.7 2.3 %copy.23 = bf16[3,2,384,384]{3,2,1,0:T(8,128)(2,1)} copy(bf16[3,2,384,384]{2,3,1,0:T(8,128)(2,1)S(1)} %bitcast.46) | data formatting | bytes 3538944 | tf_op jit(solution)/shard_map/all_to_all | solution.py:34
  148.0 4.0 %fusion.19 = bf16[512,384]{1,0:T(8,128)(2,1)S(1)} fusion(bf16[3,384,768]{2,1,0:T(8,128)(2,1)} %param.4, bf16[512,1,768]{2,0,1:T(8,128)(2,1)} %get-tuple-element.5, bf16[512,1,768]{2,0,1:T(8,128)(2,1)} %get-tuple-element.4, bf16[512,1,768]{2,0,1:T(8,128)(2,1)} %get-tuple-element.6, f32[512,384]{1,0:T(8,128)S(1)} %reduce_sum.9, ...), kind=kOutput, calls=%fused_computation.26 | convolution fusion | flops 913047552 | bytes 5701632 | tf_op jit(solution)/shard_map/tko,kio->ti/dot_general | solution.py:45
  152.0 0.4 broadcast_in_dim.8
  152.4 1.2 convert_element_type.60
  153.6 1.9 pad_maximum_fusion
  155.4 2.5 %copy.20 = bf16[512,3,768]{0,2,1:T(8,128)(2,1)} copy(bf16[512,3,768]{2,0,1:T(8,128)(2,1)S(1)} %pad_maximum_fusion) | data formatting | bytes 4718592 | tf_op jit(solution)/shard_map/stack | solution.py:35
  157.9 4.4 %fusion.10 = bf16[1,512,384]{2,1,0:T(8,128)(2,1)} fusion(bf16[512,2304]{0,1:T(8,128)(2,1)} %bitcast.45, bf16[2304,384]{1,0:T(8,128)(2,1)} %bitcast.47, f32[512,384]{1,0:T(8,128)S(1)} %reduce_sum.9), kind=kOutput, calls=%fused_computation.12 | convolution fusion | flops 906559488 | bytes 5308416 | tf_op jit(solution)/shard_map/dot_general | solution.py:36
  162.3 49.2 %collective-permute-done.4 = f32[3,384,384]{2,1,0:T(8,128)} collective-permute-done((f32[3,384,384]{2,1,0:T(8,128)}, f32[3,384,384]{2,1,0:T(8,128)}, u32[]{:S(2)}, u32[]{:S(2)}) %collective-permute-start.4) | collective-permute-done | bytes 1769504 | tf_op jit(solution)/shard_map/ppermute | solution.py:69
  211.5 3.4 %add.80 = f32[3,384,384]{2,1,0:T(8,128)} add(f32[3,384,384]{2,1,0:T(8,128)} %add.79, f32[3,384,384]{2,1,0:T(8,128)} %collective-permute-done.4) | non-fusion elementwise | flops 442368 | bytes 5308416 | tf_op jit(solution)/shard_map/add | solution.py:69
  (9 shorter events, 0.4 us)
Async XLA Ops:
  7.2 35.7 %all-gather.2.cloned.1.call-start = ((), (), s32[]{:S(2)}) async-start(), calls=%async_computation.1 | async-start | bytes 4718592 | tf_op jit(solution)/shard_map/all_gather | solution.py:32
  9.4 2.2 copy-start
  11.7 13.3 %collective-permute-start = (bf16[2,256,384]{2,1,0:T(8,128)(2,1)S(1)}, bf16[2,256,384]{2,1,0:T(8,128)(2,1)S(1)}, u32[]{:S(2)}, u32[]{:S(2)}) collective-permute-start(bf16[2,256,384]{2,1,0:T(8,128)(2,1)S(1)} %get-tuple-element.14), channel_id=1, source_target_pairs={{0,4},{4,8},{8,12},{1,5},{5,9},{9,13},{2,6},{6,10},{10,14},{3,7},{... | collective-permute-start | bytes 1179656 | tf_op jit(solution)/shard_map/ppermute | solution.py:10
  16.7 12.5 %collective-permute-start.1 = (bf16[2,256,384]{2,1,0:T(8,128)(2,1)S(1)}, bf16[2,256,384]{2,1,0:T(8,128)(2,1)S(1)}, u32[]{:S(2)}, u32[]{:S(2)}) collective-permute-start(bf16[2,256,384]{2,1,0:T(8,128)(2,1)S(1)} %get-tuple-element.15), channel_id=1, source_target_pairs={{4,0},{8,4},{12,8},{5,1},{9,5},{13,9},{6,2},{10,6},{14,10},{7,3},{... | collective-permute-start | bytes 1179656 | tf_op jit(solution)/shard_map/ppermute | solution.py:10
  47.6 1.6 copy-start.1
  50.1 40.9 %collective-permute-start.2 = (f32[3,384,384]{2,1,0:T(8,128)S(1)}, f32[3,384,384]{2,1,0:T(8,128)S(1)}, u32[]{:S(2)}, u32[]{:S(2)}) collective-permute-start(f32[3,384,384]{2,1,0:T(8,128)S(1)} %fusion.38), channel_id=1, source_target_pairs={{0,2},{2,0},{1,3},{3,1},{4,6},{6,4},{5,7},{7,5},{8,10},{10,8},{9,1... | collective-permute-start | bytes 5308424 | tf_op jit(solution)/shard_map/ppermute | solution.py:62
  91.8 40.0 %collective-permute-start.3 = (f32[3,384,384]{2,1,0:T(8,128)S(1)}, f32[3,384,384]{2,1,0:T(8,128)S(1)}, u32[]{:S(2)}, u32[]{:S(2)}) collective-permute-start(f32[3,384,384]{2,1,0:T(8,128)S(1)} %convolution_add_fusion), channel_id=1, source_target_pairs={{0,4},{4,0},{8,12},{12,8},{1,5},{5,1},{9,13},{13,9},{2,6},{6,2},{1... | collective-permute-start | bytes 5308424 | tf_op jit(solution)/shard_map/ppermute | solution.py:69
  133.2 78.3 %collective-permute-start.4 = (f32[3,384,384]{2,1,0:T(8,128)}, f32[3,384,384]{2,1,0:T(8,128)}, u32[]{:S(2)}, u32[]{:S(2)}) collective-permute-start(f32[3,384,384]{2,1,0:T(8,128)} %add.79), channel_id=1, source_target_pairs={{0,8},{4,12},{8,0},{12,4},{1,9},{5,13},{9,1},{13,5},{2,10},{6,14},... | collective-permute-start | bytes 5308424 | tf_op jit(solution)/shard_map/ppermute | solution.py:69
Sparse Core Ops, SparseCore 0:
  30.6 12.2 all-gather.1
